TPU v7x, 256 devices: a whole 4x4x8 slice. The times are simulated.
256 devices in a mesh: seg: 128 (over y, x_hi, z, core), fsdp: 2 (over x_lo).
Axes of the slice: x: 4 (x_hi: 2, x_lo: 2; x = x_hi * 2 + x_lo), y: 4, z: 8, core: 2. Of those that a mesh axis runs over, the one named last changes fastest.
Arguments:
- hidden_states: bfloat16 [98304, 2048], P(('seg', 'fsdp'))
- queries: bfloat16 [98304, 2048], P(('seg', 'fsdp'))
- w_key: bfloat16 [2048, 2048], P('fsdp')
- w_value: bfloat16 [2048, 2048], P('fsdp'), may hold values from -0.125 to 0.125
Outputs:
- attended: bfloat16 [98304, 2048], P(('seg', 'fsdp'))
All inputs are finite; a program needn't handle non-finite values.
Results may differ from a plain program's by a relative error of at most 0.0076.
Values may be sent and summed in bfloat16 or wider, within the bound.
No kernel may reach another device: no remote copies, remote signals or barrier semaphores. Data moves between devices by JAX's collectives and lax.ppermute only.
A program may use at most 128 MiB of HBM per device.

v0:
```python
import jax
import jax.numpy as jnp
from jax import lax
from jax.sharding import PartitionSpec as P

HD = 128
MEM = 2


def from_behind(value, axis, steps):
    count = lax.axis_size(axis)
    leading, last = (max(0, -steps), min(count, count - steps))
    return lax.ppermute(value, axis, [(source, source + steps) for source in range(leading, last)])


def attend_group(query_rows, key_flat, value_flat, allowed, group_number):
    span = 4 * HD
    count = query_rows.shape[0]
    query_part = lax.dynamic_slice_in_dim(query_rows, group_number * span, span, 1).reshape(
        count, 4, HD
    )
    key_part = lax.dynamic_slice_in_dim(key_flat, group_number * span, span, 1).reshape(
        key_flat.shape[0], 4, HD
    )
    value_part = lax.dynamic_slice_in_dim(value_flat, group_number * span, span, 1).reshape(
        value_flat.shape[0], 4, HD
    )
    scores = jnp.einsum(
        "qhd,khd->hqk", query_part, key_part, preferred_element_type=jnp.float32
    ) * HD ** (-0.5)
    scores = jnp.where(allowed[None], scores, jnp.float32(-1e30))
    top_score = jnp.max(scores, axis=-1, keepdims=True)
    expo = jnp.where(allowed[None], jnp.exp(scores - top_score), jnp.float32(0.0))
    total = jnp.sum(expo, axis=-1)
    weights = expo.astype(jnp.bfloat16)
    mixed = jnp.einsum("hqk,khd->qhd", weights, value_part, preferred_element_type=jnp.float32)
    mixed = mixed / jnp.transpose(total)[:, :, None]
    return mixed.reshape(count, span).astype(jnp.bfloat16)


def body(hidden_states, queries, w_key, w_value):
    tok_rows = hidden_states.shape[0]
    width = w_key.shape[1]
    key_sum = jnp.dot(
        hidden_states,
        lax.all_gather(w_key, "fsdp", axis=0, tiled=True),
        preferred_element_type=jnp.float32,
    )
    value_sum = jnp.dot(
        hidden_states,
        lax.all_gather(w_value, "fsdp", axis=0, tiled=True),
        preferred_element_type=jnp.float32,
    )
    own_pair = jnp.stack([key_sum.astype(jnp.bfloat16), value_sum.astype(jnp.bfloat16)])
    own_unit = lax.all_gather(own_pair, "fsdp", axis=1, tiled=True)
    earlier = []
    for distance in range(1, MEM + 1):
        arrived = from_behind(own_unit, "seg", distance)
        earlier.insert(0, arrived)
    context = jnp.stack(earlier + [own_unit])
    seg_rows = context.shape[2]
    key_flat = context[:, 0].reshape((MEM + 1) * seg_rows, width)
    value_flat = context[:, 1].reshape((MEM + 1) * seg_rows, width)
    seg_number = lax.axis_index("seg")
    half_number = lax.axis_index("fsdp")
    query_pos = half_number * tok_rows + jnp.arange(tok_rows, dtype=jnp.int32)
    key_pos = jnp.arange((MEM + 1) * seg_rows, dtype=jnp.int32)
    block_of = key_pos // seg_rows
    within = key_pos % seg_rows
    earlier_ok = (block_of < MEM) & (seg_number >= MEM - block_of)
    own_ok = (block_of == MEM)[None, :] & (within[None, :] <= query_pos[:, None])
    allowed = earlier_ok[None, :] | own_ok

    def one_group(group_number):
        return attend_group(queries, key_flat, value_flat, allowed, group_number)

    grouped = lax.map(one_group, jnp.arange(width // (4 * HD), dtype=jnp.int32))
    return jnp.transpose(grouped, (1, 0, 2)).reshape(tok_rows, width)


def solution(mesh):
    placed = (P(("seg", "fsdp"), None), P(("seg", "fsdp"), None), P("fsdp", None), P("fsdp", None))
    return jax.shard_map(
        body, mesh=mesh, in_specs=placed, out_specs=P(("seg", "fsdp"), None), check_vma=False
    )
```

profile of v0, /device:TPU:8, one launch (start us, length us, event | category | flops | bytes accessed | tf_op | source)
XLA Modules:
  0.0 693.0 jit_solution(751616169947207539)
XLA Ops:
  8.1 113.0 %all-gather.4.cloned.1.call-done = bf16[2048,2048]{1,0:T(8,128)(2,1)} async-done(((bf16[1024,2048]{1,0:T(8,128)(2,1)}), bf16[2048,2048]{1,0:T(8,128)(2,1)}) %all-gather.4.cloned.1.call-update) | async-done | bytes 8388624 | tf_op jit(solution)/shard_map/all_gather | solution.py:46
  121.1 6.8 fusion.22
  127.9 105.1 %all-gather.6.cloned.1.call-done = bf16[2048,2048]{1,0:T(8,128)(2,1)} async-done(((bf16[1024,2048]{1,0:T(8,128)(2,1)}), bf16[2048,2048]{1,0:T(8,128)(2,1)}) %all-gather.6.cloned.1.call-update) | async-done | bytes 8388624 | tf_op jit(solution)/shard_map/all_gather | solution.py:51
  233.0 6.8 fusion.23
  239.8 2.0 pad_maximum_fusion.1
  241.8 86.6 %all-gather.8.cloned.1.call-done = bf16[2,768,2048]{2,1,0:T(8,128)(2,1)} async-done(((bf16[2,384,2048]{2,1,0:T(8,128)(2,1)}), bf16[2,768,2048]{2,1,0:T(8,128)(2,1)}) %all-gather.8.cloned.1.call-update) | async-done | bytes 6291472 | tf_op jit(solution)/shard_map/all_gather | solution.py:55
  328.3 3.5 collective-permute-start
  331.8 2.1 collective-permute-start.1
  334.0 139.5 %collective-permute-done = bf16[2,768,2048]{2,1,0:T(8,128)(2,1)} collective-permute-done((bf16[2,768,2048]{2,1,0:T(8,128)(2,1)}, bf16[2,768,2048]{2,1,0:T(8,128)(2,1)}, u32[]{:S(2)}, u32[]{:S(2)}) %collective-permute-start) | collective-permute-done | bytes 6291488 | tf_op jit(solution)/shard_map/ppermute | solution.py:13
  473.4 66.1 %collective-permute-done.1 = bf16[2,768,2048]{2,1,0:T(8,128)(2,1)} collective-permute-done((bf16[2,768,2048]{2,1,0:T(8,128)(2,1)}, bf16[2,768,2048]{2,1,0:T(8,128)(2,1)}, u32[]{:S(2)}, u32[]{:S(2)}) %collective-permute-start.1) | collective-permute-done | bytes 6291488 | tf_op jit(solution)/shard_map/ppermute | solution.py:13
  539.6 9.6 %pad_maximum_fusion = bf16[3,2,768,2048]{3,2,1,0:T(8,128)(2,1)S(1)} fusion(bf16[1,2,768,2048]{3,2,1,0:T(8,128)(2,1)} %bitcast.62, bf16[1,2,768,2048]{3,2,1,0:T(8,128)(2,1)} %bitcast.3, bf16[1,2,768,2048]{3,2,1,0:T(8,128)(2,1)} %bitcast.2), kind=kLoop, calls=%fused_computation.21 | loop fusion | flops 18874368 | bytes 37748736 | tf_op jit(solution)/shard_map/stack | solution.py:60
  549.2 6.8 fusion.33
  555.9 127.8 %while.11 = (s32[]{:T(128)}, bf16[4,384,512]{1,2,0:T(8,128)(2,1)}, s32[4]{0:T(128)S(1)}, bf16[2304,2048]{1,0:T(8,128)(2,1)}, bf16[384,2048]{1,0:T(8,128)(2,1)}, ...) while((s32[]{:T(128)}, bf16[4,384,512]{1,2,0:T(8,128)(2,1)}, ...), condition=%wide.region_3.4_spmd.clone, body=%wide.region_0.3_spmd.clone.sunk | while | flops 1836222720 | bytes 42692296 | solution.py:77
  557.2 4.1 constant_dynamic-slice_fusion.5
  561.2 4.3 copy.24
  565.6 1.0 constant_dynamic-slice_fusion.6
  566.6 0.9 copy.23
  567.5 0.8 and_or_fusion.2
  568.3 10.5 %fusion.54 = (f32[4,384]{1,0:T(4,128)S(1)}, bf16[4,384,2304]{2,1,0:T(8,128)(2,1)}) fusion(pred[384,2304]{1,0:T(8,128)(4,1)S(1)} %and_or_fusion.2, bf16[384,4,128]{0,2,1:T(8,128)(2,1)} %bitcast.60, bf16[2304,4,128]{0,2,1:T(8,128)(2,1)} %bitcast.56), kind=kOutput, calls=%fused_computation.42.clone.1 | convolution fusion | flops 927205632 | bytes 10721280 | tf_op jit(solution)/shard_map/while/body/eval_jaxpr/sub | solution.py:33
  578.8 2.5 copy.22
  581.3 5.7 fusion.55
  587.1 0.8 constant_dynamic-update-slice_fusion.2
  589.1 4.1 constant_dynamic-slice_fusion.5
  593.2 4.3 copy.24
  597.5 1.0 constant_dynamic-slice_fusion.6
  598.5 0.9 copy.23
  599.5 0.8 and_or_fusion.2
  600.2 10.5 %fusion.54 = (f32[4,384]{1,0:T(4,128)S(1)}, bf16[4,384,2304]{2,1,0:T(8,128)(2,1)}) fusion(pred[384,2304]{1,0:T(8,128)(4,1)S(1)} %and_or_fusion.2, bf16[384,4,128]{0,2,1:T(8,128)(2,1)} %bitcast.60, bf16[2304,4,128]{0,2,1:T(8,128)(2,1)} %bitcast.56), kind=kOutput, calls=%fused_computation.42.clone.1 | convolution fusion | flops 927205632 | bytes 10721280 | tf_op jit(solution)/shard_map/while/body/eval_jaxpr/sub | solution.py:33
  610.7 2.5 copy.22
  613.3 5.7 fusion.55
  619.0 0.8 constant_dynamic-update-slice_fusion.2
  621.0 4.1 constant_dynamic-slice_fusion.5
  625.1 4.3 copy.24
  629.5 1.0 constant_dynamic-slice_fusion.6
  630.5 0.9 copy.23
  632.2 10.5 %fusion.54 = (f32[4,384]{1,0:T(4,128)S(1)}, bf16[4,384,2304]{2,1,0:T(8,128)(2,1)}) fusion(pred[384,2304]{1,0:T(8,128)(4,1)S(1)} %and_or_fusion.2, bf16[384,4,128]{0,2,1:T(8,128)(2,1)} %bitcast.60, bf16[2304,4,128]{0,2,1:T(8,128)(2,1)} %bitcast.56), kind=kOutput, calls=%fused_computation.42.clone.1 | convolution fusion | flops 927205632 | bytes 10721280 | tf_op jit(solution)/shard_map/while/body/eval_jaxpr/sub | solution.py:33
  642.7 2.5 copy.22
  645.2 5.8 fusion.55
  651.0 0.8 constant_dynamic-update-slice_fusion.2
  653.0 4.1 constant_dynamic-slice_fusion.5
  657.1 4.3 copy.24
  661.4 1.0 constant_dynamic-slice_fusion.6
  662.5 0.9 copy.23
  664.1 10.5 %fusion.54 = (f32[4,384]{1,0:T(4,128)S(1)}, bf16[4,384,2304]{2,1,0:T(8,128)(2,1)}) fusion(pred[384,2304]{1,0:T(8,128)(4,1)S(1)} %and_or_fusion.2, bf16[384,4,128]{0,2,1:T(8,128)(2,1)} %bitcast.60, bf16[2304,4,128]{0,2,1:T(8,128)(2,1)} %bitcast.56), kind=kOutput, calls=%fused_computation.42.clone.1 | convolution fusion | flops 927205632 | bytes 10721280 | tf_op jit(solution)/shard_map/while/body/eval_jaxpr/sub | solution.py:33
  674.6 2.5 copy.22
  677.2 5.7 fusion.55
  682.9 0.8 constant_dynamic-update-slice_fusion.2
  683.7 2.7 copy.15
  (21 shorter events, 5.4 us)
Async XLA Ops:
  6.5 114.6 %copy-start = (bf16[384,2048]{1,0:T(8,128)(2,1)S(1)}, bf16[384,2048]{1,0:T(8,128)(2,1)}, u32[]{:S(2)}) copy-start(bf16[384,2048]{1,0:T(8,128)(2,1)} %param.6) | copy-start | bytes 4718596
  6.5 114.6 %all-gather.4.cloned.1.call-start = ((), (), s32[]{:S(2)}) async-start(), calls=%async_computation | async-start | bytes 12582912 | tf_op jit(solution)/shard_map/all_gather | solution.py:46
  7.3 225.7 %all-gather.6.cloned.1.call-start = ((), (), s32[]{:S(2)}) async-start(), calls=%async_computation.1 | async-start | bytes 12582912 | tf_op jit(solution)/shard_map/all_gather | solution.py:51
  8.0 320.3 %all-gather.8.cloned.1.call-start = ((), (), s32[]{:S(2)}) async-start(), calls=%async_computation.2 | async-start | bytes 9437184 | tf_op jit(solution)/shard_map/all_gather | solution.py:55
  328.3 145.1 %collective-permute-start = (bf16[2,768,2048]{2,1,0:T(8,128)(2,1)}, bf16[2,768,2048]{2,1,0:T(8,128)(2,1)}, u32[]{:S(2)}, u32[]{:S(2)}) collective-permute-start(bf16[2,768,2048]{2,1,0:T(8,128)(2,1)} %all-gather.8.cloned.1.call-done), channel_id=1, source_target_pairs={{0,4},{2,6},{4,8},{6,10},{8,12},{10,14},{12,16},{14,18},{16,20},{1... | collective-permute-start | bytes 18874376 | tf_op jit(solution)/shard_map/ppermute | solution.py:13
  331.8 207.8 %collective-permute-start.1 = (bf16[2,768,2048]{2,1,0:T(8,128)(2,1)}, bf16[2,768,2048]{2,1,0:T(8,128)(2,1)}, u32[]{:S(2)}, u32[]{:S(2)}) collective-permute-start(bf16[2,768,2048]{2,1,0:T(8,128)(2,1)} %all-gather.8.cloned.1.call-done), channel_id=1, source_target_pairs={{0,2},{2,4},{4,6},{6,8},{8,10},{10,12},{12,14},{14,16},{16,18},{18... | collective-permute-start | bytes 18874376 | tf_op jit(solution)/shard_map/ppermute | solution.py:13
  683.7 2.7 copy-start.1
Sparse Core Ops, SparseCore 0:
  9.1 111.9 all-gather.3
  122.9 110.0 all-gather.5
  241.9 86.4 all-gather.7
where the time goes:
time: 694 us; the launch traced here: 693 us
  waiting for transfers between devices  512 us (74%)
  matrix products  78.6 us (11%)
  local copies, waits for them, and re-layouts  66.5 us (10%)
  other arithmetic  14.6 us (2%)
  between operations  13.2 us (2%)
    ppermute x2, waiting for transfers between devices, from_behind(): lax.ppermute(value, axis, [(source, source + steps) for source in range(l...  206 us
    all_gather x1, waiting for transfers between devices, body(): lax.all_gather(w_key, 'fsdp', axis=0, tiled=True)  113 us
    all_gather x1, waiting for transfers between devices, body(): lax.all_gather(w_value, 'fsdp', axis=0, tiled=True)  105 us
    all_gather x1, waiting for transfers between devices, body(): own_unit = lax.all_gather(own_pair, 'fsdp', axis=1, tiled=True)  86.6 us
    sub x4, matrix products, attend_group(): scores - top_score  42 us
    dynamic_slice x8, local copies, waits for them, and re-layouts, attend_group(): lax.dynamic_slice_in_dim(key_flat, group_number * span, span, 1)  33.7 us
    dot_general x4, matrix products, attend_group(): jnp.einsum('hqk,khd->qhd', weights, value_part, preferred_element_type=jn...  23 us
  transfers between devices with their start and end apart: 5, of which 5 were waited for; matrix products, arithmetic and copies ran while one was open for 1% of the time, Pallas kernels for 0%

commit v1 on v0

--- a/solution.py
+++ b/solution.py
@@ -5,6 +5,12 @@
 
 HD = 128
 MEM = 2
+_recover_trees = lambda block_in, along_axis: jnp.concatenate(
+    lax.all_to_all(
+        jnp.stack([block_in for _ in range(lax.axis_size(along_axis))], axis=0), along_axis, 0, 0
+    ),
+    0,
+)
 
 
 def from_behind(value, axis, steps):
@@ -47,9 +53,7 @@
         preferred_element_type=jnp.float32,
     )
     value_sum = jnp.dot(
-        hidden_states,
-        lax.all_gather(w_value, "fsdp", axis=0, tiled=True),
-        preferred_element_type=jnp.float32,
+        hidden_states, _recover_trees(w_value, "fsdp"), preferred_element_type=jnp.float32
     )
     own_pair = jnp.stack([key_sum.astype(jnp.bfloat16), value_sum.astype(jnp.bfloat16)])
     own_unit = lax.all_gather(own_pair, "fsdp", axis=1, tiled=True)

time: 694 us -> 665 us (0.958)
  waiting for transfers between devices: 512 us -> 299 us
  blocking collectives: 0 us -> 179 us
  other arithmetic: 14.6 us -> 22.1 us
    all_to_all x0 -> x1, blocking collectives: none -> 179 us  [lax.all_to_all(jnp.stack([block_in for _ in range(lax.axis_size(along_axi...]
    all_gather x1, waiting for transfers between devices: 113 us -> 4.6 us  [body(): lax.all_gather(w_key, 'fsdp', axis=0, tiled=True)]
    all_gather x1 -> x0, waiting for transfers between devices: 105 us -> none  [body(): lax.all_gather(w_value, 'fsdp', axis=0, tiled=True)]
    another operation x0 -> x1, other arithmetic: none -> 7.46 us  [jnp.stack([block_in for _ in range(lax.axis_size(along_axis))], axis=0)]
  transfers between devices with their start and end apart: 5 -> 4, of which waited for: 5 -> 4; matrix products, arithmetic and copies ran while one was open for 1% -> 2% of each run, Pallas kernels for 0% -> 0%
where the time goes in v1:
time: 665 us; the launch traced here: 664 us
  waiting for transfers between devices  299 us (45%)
  blocking collectives  179 us (27%)
  matrix products  75.2 us (11%)
  local copies, waits for them, and re-layouts  66.6 us (10%)
  other arithmetic  22.1 us (3%)
  between operations  13.5 us (2%)
    ppermute x2, waiting for transfers between devices, from_behind(): lax.ppermute(value, axis, [(source, source + steps) for source in range(l...  206 us
    all_to_all x1, blocking collectives, lax.all_to_all(jnp.stack([block_in for _ in range(lax.axis_size(along_axi...  179 us
    all_gather x1, waiting for transfers between devices, body(): own_unit = lax.all_gather(own_pair, 'fsdp', axis=1, tiled=True)  88.5 us
    sub x4, matrix products, attend_group(): scores - top_score  42 us
    dynamic_slice x8, local copies, waits for them, and re-layouts, attend_group(): lax.dynamic_slice_in_dim(key_flat, group_number * span, span, 1)  33.7 us
    dot_general x4, matrix products, attend_group(): jnp.einsum('hqk,khd->qhd', weights, value_part, preferred_element_type=jn...  23 us
  transfers between devices with their start and end apart: 4, of which 4 were waited for; matrix products, arithmetic and copies ran while one was open for 2% of the time, Pallas kernels for 0%

profile of v1, /device:TPU:8, one launch (start us, length us, event | category | flops | bytes accessed | tf_op | source)
XLA Modules:
  0.0 664.4 jit_solution(13451190703903012209)
XLA Ops:
  7.3 7.5 %pad_maximum_fusion.1 = bf16[2,1024,2048]{2,1,0:T(8,128)(2,1)} fusion(bf16[1,1024,2048]{2,1,0:T(8,128)(2,1)} %bitcast.68), kind=kLoop, calls=%fused_computation.22 | loop fusion | flops 4194304 | bytes 12582912 | tf_op jit(solution)/shard_map/stack | solution.py:10
  14.8 179.3 %all_to_all.5 = bf16[2,1024,2048]{2,1,0:T(8,128)(2,1)S(1)} all-to-all(bf16[2,1024,2048]{2,1,0:T(8,128)(2,1)} %pad_maximum_fusion.1), channel_id=1, replica_groups=mesh['seg'=128,'fsdp'=2] {'fsdp'}, dimensions={0} | all-to-all | bytes 16777216 | tf_op jit(solution)/shard_map/all_to_all | solution.py:9
  194.1 3.4 fusion.23
  197.5 4.6 all-gather.3.cloned.1.call-done
  202.1 6.8 %fusion.22 = bf16[1,384,2048]{2,1,0:T(8,128)(2,1)S(1)} fusion(bf16[384,2048]{1,0:T(8,128)(2,1)S(1)} %copy-done, bf16[2048,2048]{1,0:T(8,128)(2,1)} %all-gather.3.cloned.1.call-done), kind=kOutput, calls=%fused_computation.26 | convolution fusion | flops 3222011904 | bytes 11534336 | tf_op jit(solution)/shard_map/dot_general | solution.py:50
  208.9 2.0 pad_maximum_fusion.2
  210.9 88.5 %all-gather.5.cloned.1.call-done = bf16[2,768,2048]{2,1,0:T(8,128)(2,1)} async-done(((bf16[2,384,2048]{2,1,0:T(8,128)(2,1)}), bf16[2,768,2048]{2,1,0:T(8,128)(2,1)}) %all-gather.5.cloned.1.call-update) | async-done | bytes 6291472 | tf_op jit(solution)/shard_map/all_gather | solution.py:59
  299.4 3.5 collective-permute-start
  302.8 2.1 collective-permute-start.1
  305.0 139.5 %collective-permute-done = bf16[2,768,2048]{2,1,0:T(8,128)(2,1)} collective-permute-done((bf16[2,768,2048]{2,1,0:T(8,128)(2,1)}, bf16[2,768,2048]{2,1,0:T(8,128)(2,1)}, u32[]{:S(2)}, u32[]{:S(2)}) %collective-permute-start) | collective-permute-done | bytes 6291488 | tf_op jit(solution)/shard_map/ppermute | solution.py:19
  444.5 66.1 %collective-permute-done.1 = bf16[2,768,2048]{2,1,0:T(8,128)(2,1)} collective-permute-done((bf16[2,768,2048]{2,1,0:T(8,128)(2,1)}, bf16[2,768,2048]{2,1,0:T(8,128)(2,1)}, u32[]{:S(2)}, u32[]{:S(2)}) %collective-permute-start.1) | collective-permute-done | bytes 6291488 | tf_op jit(solution)/shard_map/ppermute | solution.py:19
  510.6 9.6 %pad_maximum_fusion = bf16[3,2,768,2048]{3,2,1,0:T(8,128)(2,1)S(1)} fusion(bf16[1,2,768,2048]{3,2,1,0:T(8,128)(2,1)} %bitcast.67, bf16[1,2,768,2048]{3,2,1,0:T(8,128)(2,1)} %bitcast.6, bf16[1,2,768,2048]{3,2,1,0:T(8,128)(2,1)} %bitcast.5), kind=kLoop, calls=%fused_computation.21 | loop fusion | flops 18874368 | bytes 37748736 | tf_op jit(solution)/shard_map/stack | solution.py:64
  520.2 6.7 %fusion.33 = (bf16[3,1,768,2048]{3,2,1,0:T(8,128)(2,1)}, bf16[3,1,768,2048]{3,2,1,0:T(8,128)(2,1)}) fusion(bf16[3,2,768,2048]{3,2,1,0:T(8,128)(2,1)S(1)} %pad_maximum_fusion), kind=kLoop, calls=%fused_computation.44 | loop fusion | bytes 37748736 | tf_op jit(solution)/shard_map/slice | solution.py:66
  526.9 128.0 %while.11 = (s32[]{:T(128)}, bf16[4,384,512]{1,2,0:T(8,128)(2,1)}, s32[4]{0:T(128)S(1)}, bf16[2304,2048]{1,0:T(8,128)(2,1)}, bf16[384,2048]{1,0:T(8,128)(2,1)}, ...) while((s32[]{:T(128)}, bf16[4,384,512]{1,2,0:T(8,128)(2,1)}, ...), condition=%wide.region_3.4_spmd.clone, body=%wide.region_0.3_spmd.clone.sunk | while | flops 1836222720 | bytes 42692296 | solution.py:81
  528.2 4.1 constant_dynamic-slice_fusion.5
  532.3 4.3 copy.27
  536.6 1.0 constant_dynamic-slice_fusion.6
  537.6 0.9 copy.26
  538.6 0.8 and_or_fusion.2
  539.3 10.5 %fusion.54 = (f32[4,384]{1,0:T(4,128)S(1)}, bf16[4,384,2304]{2,1,0:T(8,128)(2,1)}) fusion(pred[384,2304]{1,0:T(8,128)(4,1)S(1)} %and_or_fusion.2, bf16[384,4,128]{0,2,1:T(8,128)(2,1)} %bitcast.64, bf16[2304,4,128]{0,2,1:T(8,128)(2,1)} %bitcast.60), kind=kOutput, calls=%fused_computation.43.clone.1 | convolution fusion | flops 927205632 | bytes 10721280 | tf_op jit(solution)/shard_map/while/body/eval_jaxpr/sub | solution.py:39
  549.8 2.5 copy.25
  552.4 5.7 fusion.55
  558.1 0.8 constant_dynamic-update-slice_fusion.2
  560.2 4.1 constant_dynamic-slice_fusion.5
  564.3 4.3 copy.27
  568.6 1.0 constant_dynamic-slice_fusion.6
  569.6 0.9 copy.26
  571.3 10.5 %fusion.54 = (f32[4,384]{1,0:T(4,128)S(1)}, bf16[4,384,2304]{2,1,0:T(8,128)(2,1)}) fusion(pred[384,2304]{1,0:T(8,128)(4,1)S(1)} %and_or_fusion.2, bf16[384,4,128]{0,2,1:T(8,128)(2,1)} %bitcast.64, bf16[2304,4,128]{0,2,1:T(8,128)(2,1)} %bitcast.60), kind=kOutput, calls=%fused_computation.43.clone.1 | convolution fusion | flops 927205632 | bytes 10721280 | tf_op jit(solution)/shard_map/while/body/eval_jaxpr/sub | solution.py:39
  581.8 2.5 copy.25
  584.4 5.8 fusion.55
  590.1 0.8 constant_dynamic-update-slice_fusion.2
  592.1 4.1 constant_dynamic-slice_fusion.5
  596.2 4.3 copy.27
  600.6 1.0 constant_dynamic-slice_fusion.6
  601.6 0.9 copy.26
  603.3 10.5 %fusion.54 = (f32[4,384]{1,0:T(4,128)S(1)}, bf16[4,384,2304]{2,1,0:T(8,128)(2,1)}) fusion(pred[384,2304]{1,0:T(8,128)(4,1)S(1)} %and_or_fusion.2, bf16[384,4,128]{0,2,1:T(8,128)(2,1)} %bitcast.64, bf16[2304,4,128]{0,2,1:T(8,128)(2,1)} %bitcast.60), kind=kOutput, calls=%fused_computation.43.clone.1 | convolution fusion | flops 927205632 | bytes 10721280 | tf_op jit(solution)/shard_map/while/body/eval_jaxpr/sub | solution.py:39
  613.8 2.5 copy.25
  616.3 5.8 fusion.55
  622.1 0.8 constant_dynamic-update-slice_fusion.2
  624.1 4.1 constant_dynamic-slice_fusion.5
  628.2 4.3 copy.27
  632.6 1.0 constant_dynamic-slice_fusion.6
  633.6 0.9 copy.26
  635.3 10.5 %fusion.54 = (f32[4,384]{1,0:T(4,128)S(1)}, bf16[4,384,2304]{2,1,0:T(8,128)(2,1)}) fusion(pred[384,2304]{1,0:T(8,128)(4,1)S(1)} %and_or_fusion.2, bf16[384,4,128]{0,2,1:T(8,128)(2,1)} %bitcast.64, bf16[2304,4,128]{0,2,1:T(8,128)(2,1)} %bitcast.60), kind=kOutput, calls=%fused_computation.43.clone.1 | convolution fusion | flops 927205632 | bytes 10721280 | tf_op jit(solution)/shard_map/while/body/eval_jaxpr/sub | solution.py:39
  645.8 2.5 copy.25
  648.3 5.7 fusion.55
  654.1 0.8 constant_dynamic-update-slice_fusion.2
  654.9 2.7 copy.18
  (20 shorter events, 5.4 us)
Async XLA Ops:
  6.5 187.6 %copy-start = (bf16[384,2048]{1,0:T(8,128)(2,1)S(1)}, bf16[384,2048]{1,0:T(8,128)(2,1)}, u32[]{:S(2)}) copy-start(bf16[384,2048]{1,0:T(8,128)(2,1)} %param.6) | copy-start | bytes 4718596
  6.5 195.6 %all-gather.3.cloned.1.call-start = ((), (), s32[]{:S(2)}) async-start(), calls=%async_computation.1 | async-start | bytes 12582912 | tf_op jit(solution)/shard_map/all_gather | solution.py:52
  7.3 292.1 %all-gather.5.cloned.1.call-start = ((), (), s32[]{:S(2)}) async-start(), calls=%async_computation.2 | async-start | bytes 9437184 | tf_op jit(solution)/shard_map/all_gather | solution.py:59
  299.4 145.1 %collective-permute-start = (bf16[2,768,2048]{2,1,0:T(8,128)(2,1)}, bf16[2,768,2048]{2,1,0:T(8,128)(2,1)}, u32[]{:S(2)}, u32[]{:S(2)}) collective-permute-start(bf16[2,768,2048]{2,1,0:T(8,128)(2,1)} %all-gather.5.cloned.1.call-done), channel_id=1, source_target_pairs={{0,4},{2,6},{4,8},{6,10},{8,12},{10,14},{12,16},{14,18},{16,20},{1... | collective-permute-start | bytes 18874376 | tf_op jit(solution)/shard_map/ppermute | solution.py:19
  302.8 207.8 %collective-permute-start.1 = (bf16[2,768,2048]{2,1,0:T(8,128)(2,1)}, bf16[2,768,2048]{2,1,0:T(8,128)(2,1)}, u32[]{:S(2)}, u32[]{:S(2)}) collective-permute-start(bf16[2,768,2048]{2,1,0:T(8,128)(2,1)} %all-gather.5.cloned.1.call-done), channel_id=1, source_target_pairs={{0,2},{2,4},{4,6},{6,8},{8,10},{10,12},{12,14},{14,16},{16,18},{18... | collective-permute-start | bytes 18874376 | tf_op jit(solution)/shard_map/ppermute | solution.py:19
  654.9 2.7 copy-start.1
Sparse Core Ops, SparseCore 0:
  9.1 192.9 all-gather.2
  211.0 88.2 all-gather.4
